TPU v7x, 512 devices: a whole 4x4x16 slice. The times are simulated.
512 devices in a mesh: grp: 16 (over z), wrk: 32 (over y, x, core).
Axes of the slice: x: 4, y: 4, z: 16, core: 2. Of those that a mesh axis runs over, the one named last changes fastest.
Arguments:
- orbitals: bfloat16 [512, 32, 1024], P(('grp', 'wrk')), may hold values from -6 to 6
- offsets: int32 [512, 3], replicated, may hold values from 0 to 135, as said below
- pair_slots: int32 [16, 32, 6, 2], P('grp', 'wrk'), may hold values from 0 to 511, as said below
- pair_count: int32 [16, 32], P('grp', 'wrk'), may hold values from 0 to 6, as said below
Outputs:
- exchange_fields: float32 [512, 32, 1024], P(('grp', 'wrk'))
Inputs may be any that keep to these rules, and one draw needn't show every extreme that they name: Row o gives the grid point of the first cell of orbital o's box; offsets of orbitals of the same or adjacent groups differ by less than 32 in each coordinate. Every slot of pair_slots[g, w] holds an orbital a of group g (numbers g * 32 to g * 32 + 31) and an orbital b other than a of group g or g + 1, with offsets of a and b differing by less than 32 in each coordinate; slots at or past pair_count[g, w] hold entries of the same kind that are not pairs. `pair_count`: the counts of every group sum to 96; in every group one worker has 6 pairs and one has none.
All inputs are finite; a program needn't handle non-finite values.
Results may differ from a plain program's by a relative error of at most 0.0003.
Values may be sent and summed in bfloat16 or wider, within the bound.
No kernel may reach another device: no remote copies, remote signals or barrier semaphores. Data moves between devices by JAX's collectives and lax.ppermute only.
A program may use at most 64 MiB of HBM per device.

v0:
```python
import jax
import jax.numpy as jnp
from jax import lax
from jax.sharding import PartitionSpec as P

screen_shift = 0.05
highest = lax.Precision.HIGHEST
EXCHANGE = "all_to_all"


def passed_along(value, axis, steps):
    count = lax.axis_size(axis)
    initial, last = (max(0, -steps), min(count, count - steps))
    return lax.ppermute(value, axis, [(source, source + steps) for source in range(initial, last)])


def sine_table(box_edge):
    counting = jnp.arange(box_edge, dtype=jnp.float32) + 1.0
    scaling = jnp.sqrt(2.0 / (box_edge + 1.0))
    return scaling * jnp.sin(jnp.pi * counting[:, None] * counting[None, :] / (box_edge + 1.0))


def inverse_symbol(box_edge):
    counting = jnp.arange(box_edge, dtype=jnp.float32) + 1.0
    eigen_one = 4.0 * jnp.sin(jnp.pi * counting / (2.0 * (box_edge + 1.0))) ** 2
    eigen_sum = eigen_one[:, None, None] + eigen_one[None, :, None] + eigen_one[None, None, :]
    return 1.0 / (eigen_sum + screen_shift)


def shift_matrices(offset_diff, box_edge):
    cell = jnp.arange(box_edge, dtype=jnp.int32)
    row_shift = cell[None, None, :] == cell[None, :, None] - offset_diff[:, 0, None, None]
    plane = jnp.arange(box_edge * box_edge, dtype=jnp.int32)
    out_y = (plane // box_edge)[None, :, None]
    out_z = (plane % box_edge)[None, :, None]
    in_y = (plane // box_edge)[None, None, :]
    in_z = (plane % box_edge)[None, None, :]
    plane_shift = (in_y == out_y - offset_diff[:, 1, None, None]) & (
        in_z == out_z - offset_diff[:, 2, None, None]
    )
    return (row_shift.astype(jnp.float32), plane_shift.astype(jnp.bfloat16))


def move_bf16(boxes, row_shift, plane_shift):
    planes = jnp.einsum("pxc,pyc->pxy", boxes, plane_shift, preferred_element_type=jnp.float32)
    return jnp.einsum("pxa,pac->pxc", row_shift, planes, precision=highest)


def unmove_f32(fields, row_shift, plane_shift):
    rows = jnp.einsum("pax,pac->pxc", row_shift, fields, precision=highest)
    high = lax.reduce_precision(rows, exponent_bits=8, mantissa_bits=7)
    rest = rows - high
    middle = lax.reduce_precision(rest, exponent_bits=8, mantissa_bits=7)
    low = rest - middle
    parts = jnp.concatenate([high, middle, low], axis=1).astype(jnp.bfloat16)
    moved = jnp.einsum("pxc,pcy->pxy", parts, plane_shift, preferred_element_type=jnp.float32)
    box_edge = fields.shape[1]
    return moved[:, :box_edge] + moved[:, box_edge : 2 * box_edge] + moved[:, 2 * box_edge :]


def solve_boxes(density, sine_rows, plane_sines, symbol):
    count_boxes, box_edge, plane_size = density.shape

    def apply_sines(field_block):
        along_first = jnp.einsum("kx,nxf->nkf", sine_rows, field_block, precision=highest)
        flat_rows = along_first.reshape(count_boxes * box_edge, plane_size)
        along_plane = jnp.dot(
            flat_rows, plane_sines, precision=highest, preferred_element_type=jnp.float32
        )
        return along_plane.reshape(count_boxes, box_edge, plane_size)

    spectrum = apply_sines(density) * symbol
    return apply_sines(spectrum)


def corner_of(orbital, offsets):
    listing = jnp.arange(offsets.shape[0], dtype=jnp.int32)
    chosen = orbital[:, None] == listing[None, :]
    return jnp.sum(jnp.where(chosen[:, :, None], offsets[None, :, :], 0), axis=1, dtype=jnp.int32)


def rows_to_orbitals(fields, rows, count):
    chosen = rows[:, None] == jnp.arange(count, dtype=jnp.int32)[None, :]
    return jnp.sum(jnp.where(chosen[:, :, None, None], fields[:, None, :, :], 0.0), axis=0)


def local(orbitals, offsets, pair_slots, pair_count):
    orb_dev, box_edge, plane_size = orbitals.shape
    workers = lax.axis_size("wrk")
    group_index = lax.axis_index("grp")
    grp_orbs = orb_dev * workers
    own_set = lax.all_gather(orbitals, "wrk", axis=0, tiled=True)
    upper_set = lax.all_gather(passed_along(orbitals, "grp", -1), "wrk", axis=0, tiled=True)
    group_set = jnp.concatenate([own_set, upper_set], axis=0)
    pair_list = pair_slots[0, 0]
    slot_cap = pair_list.shape[0]
    weights = (jnp.arange(slot_cap, dtype=jnp.int32) < pair_count[0, 0]).astype(jnp.float32)
    left_orb = pair_list[:, 0]
    right_orb = pair_list[:, 1]
    offset_diff = corner_of(right_orb, offsets) - corner_of(left_orb, offsets)
    base = group_index * grp_orbs
    left_row = jnp.clip(left_orb - base, 0, 2 * grp_orbs - 1)
    right_row = jnp.clip(right_orb - base, 0, 2 * grp_orbs - 1)
    left_boxes = jnp.take(group_set, left_row, axis=0)
    right_boxes = jnp.take(group_set, right_row, axis=0)
    row_shift, plane_shift = shift_matrices(offset_diff, box_edge)
    right_field = move_bf16(right_boxes, row_shift, plane_shift)
    sine_rows = sine_table(box_edge)
    plane_sines = (sine_rows[:, None, :, None] * sine_rows[None, :, None, :]).reshape(
        plane_size, plane_size
    )
    symbol = inverse_symbol(box_edge).reshape(box_edge, plane_size)
    left_field = left_boxes.astype(jnp.float32)
    potential = solve_boxes(left_field * right_field, sine_rows, plane_sines, symbol)
    weighted = potential * weights[:, None, None]
    to_left = weighted * right_field
    to_right = unmove_f32(weighted * left_field, row_shift, plane_shift)
    upper = right_row >= grp_orbs
    sent_fields = jnp.where(upper[:, None, None], to_right, 0.0)
    sent_rows = jnp.where(upper, right_row - grp_orbs, 0)
    got_fields = passed_along(sent_fields, "grp", 1)
    got_rows = passed_along(sent_rows, "grp", 1)
    kept_right = jnp.where(upper[:, None, None], 0.0, to_right)
    kept_rows = jnp.where(upper, 0, right_row)
    fields = jnp.concatenate([to_left, kept_right, got_fields], axis=0)
    rows = jnp.concatenate([left_row, kept_rows, got_rows], axis=0)
    combined = rows_to_orbitals(fields, rows, grp_orbs)
    if EXCHANGE == "all_to_all":
        pieces = lax.all_to_all(combined, "wrk", 0, 0, tiled=True)
        return jnp.sum(pieces, axis=0, keepdims=True)
    return lax.psum_scatter(combined, "wrk", scatter_dimension=0, tiled=True)


def solution(mesh):
    return jax.shard_map(
        local,
        mesh=mesh,
        in_specs=(P(("grp", "wrk"), None, None), P(), P("grp", "wrk", None, None), P("grp", "wrk")),
        out_specs=P(("grp", "wrk"), None, None),
        check_vma=False,
    )
```

profile of v0, /device:TPU:1, one launch (start us, length us, event | category | flops | bytes accessed | tf_op | source)
XLA Modules:
  0.0 274.2 jit_solution(15588823203964607802)
XLA Ops:
  6.5 0.0 all-gather.3.cloned.1.call-start
  6.5 0.7 all-gather.3.cloned.1.call-update
  7.3 0.0 all-gather.5.cloned.1.call-start
  7.3 1.3 collective-permute-start.1
  8.6 0.1 sine_multiply_fusion
  8.8 4.8 %collective-permute-done.1 = bf16[1,32,1024]{2,1,0:T(8,128)(2,1)S(1)} collective-permute-done((bf16[1,32,1024]{2,1,0:T(8,128)(2,1)}, bf16[1,32,1024]{2,1,0:T(8,128)(2,1)S(1)}, u32[]{:S(2)}, u32[]{:S(2)}) %collective-permute-start.1) | collective-permute-done | bytes 65568 | tf_op jit(solution)/shard_map/ppermute | solution.py:14
  13.5 0.0 copy-start.1
  13.5 0.6 copy-done.1
  14.2 0.0 all-gather.5.cloned.1.call-update
  14.2 8.0 %broadcast_multiply_fusion = f32[32,32,32,32]{3,2,1,0:T(8,128)} fusion(f32[32,32]{1,0:T(8,128)S(1)} %sine_multiply_fusion), kind=kLoop, calls=%fused_computation.14 | loop fusion | flops 1048576 | bytes 4198400 | tf_op jit(solution)/shard_map/mul | solution.py:109
  22.2 0.0 copy-start.3
  22.2 0.0 copy-start.2
  22.2 13.7 %reshape.409 = f32[1024,1024,1]{1,0,2:T(8,128)} reshape(f32[32,32,32,32]{3,2,1,0:T(8,128)} %broadcast_multiply_fusion) | data formatting | bytes 8388608 | tf_op jit(solution)/shard_map/mul | solution.py:109
  35.9 0.1 broadcast_add_fusion
  36.0 0.2 add.123
  36.2 0.2 add.124
  36.5 0.1 add.125
  37.2 0.0 copy-done.3
  37.2 0.1 iota_compare_fusion.3
  37.3 0.0 copy-done.2
  37.3 0.2 select_reduce_fusion.1
  37.6 0.1 iota_subtract_fusion
  37.7 0.1 broadcast_subtract_fusion
  37.8 0.1 broadcast_subtract_fusion.1
  37.9 37.2 %all-gather.3.cloned.1.call-done = bf16[32,32,1024]{2,1,0:T(8,128)(2,1)} async-done(((bf16[1,32,1024]{2,1,0:T(8,128)(2,1)}), bf16[32,32,1024]{2,1,0:T(8,128)(2,1)}) %all-gather.3.cloned.1.call-update) | async-done | bytes 2097168 | tf_op jit(solution)/shard_map/all_gather | solution.py:92
  75.1 3.2 %constant_dynamic-update-slice_fusion.1 = bf16[64,32,1024]{2,1,0:T(8,128)(2,1)} fusion(bf16[32,32,1024]{2,1,0:T(8,128)(2,1)} %all-gather.3.cloned.1.call-done), kind=kLoop, calls=%fused_computation.79 | loop fusion | bytes 4194304
  78.3 58.3 %all-gather.5.cloned.1.call-done = bf16[32,32,1024]{2,1,0:T(8,128)(2,1)} async-done(((bf16[1,32,1024]{2,1,0:T(8,128)(2,1)}), bf16[32,32,1024]{2,1,0:T(8,128)(2,1)}) %all-gather.5.cloned.1.call-update) | async-done | bytes 2097168 | tf_op jit(solution)/shard_map/all_gather | solution.py:93
  136.6 3.2 %constant_dynamic-update-slice_fusion = bf16[64,32,1024]{2,1,0:T(8,128)(2,1)} fusion(bf16[64,32,1024]{2,1,0:T(8,128)(2,1)} %constant_dynamic-update-slice_fusion.1, bf16[32,32,1024]{2,1,0:T(8,128)(2,1)} %all-gather.5.cloned.1.call-done), kind=kLoop, calls=%fused_computation.78 | loop fusion | bytes 4194304 | tf_op jit(solution)/shard_map/concatenate | solution.py:94
  139.8 2.8 %gather_fusion.1 = bf16[6,32,1024]{2,1,0:T(8,128)(2,1)S(1)} fusion(bf16[64,32,1024]{2,1,0:T(8,128)(2,1)} %constant_dynamic-update-slice_fusion, s32[1024]{0:T(1024)S(1)} %pad_clamp_fusion), kind=kCustom, calls=%fused_computation.1.clone | custom fusion | bytes 786456 | tf_op jit(solution)/shard_map/jit(_take)/gather | solution.py:105
  142.5 2.8 %gather_fusion = bf16[6,32,1024]{2,1,0:T(8,128)(2,1)S(1)} fusion(bf16[64,32,1024]{2,1,0:T(8,128)(2,1)} %constant_dynamic-update-slice_fusion, s32[1024]{0:T(1024)S(1)} %pad_clamp_fusion.1), kind=kCustom, calls=%fused_computation.clone | custom fusion | bytes 786456 | tf_op jit(solution)/shard_map/jit(_take)/gather | solution.py:104
  145.3 0.0 copy-start
  145.3 7.0 %fusion.1 = f32[6,32,1024]{2,1,0:T(8,128)S(1)} fusion(s32[6,1024]{1,0:T(8,128)S(1)} %broadcast_subtract_fusion, s32[1024]{0:T(1024)S(1)} %get-tuple-element.30, s32[6,1024]{1,0:T(8,128)S(1)} %broadcast_subtract_fusion.1, s32[1024]{0:T(1024)S(1)} %get-tuple-element.31, bf16[6,32,1024]{2,1,0:T(8,128)(2,1)S(1)} %gather_fusion.1, ...), kind=kOutput, calls=%fused_computation.5 | convolution fusion | flops 421724160 | bytes 1236998 | tf_op jit(solution)/shard_map/pxc,pyc->pxy/dot_general | solution.py:45
  152.3 0.5 fusion.20
  152.8 1.0 convolution_bitcast_fusion.1
  153.8 0.0 copy-done
  153.9 2.9 %convolution_multiply_fusion.1 = f32[6,32,1024]{2,1,0:T(8,128)S(1)} fusion(f32[6,32,1024]{2,1,0:T(8,128)S(1)} %convolution_bitcast_fusion.1, f32[1024,1024,1]{1,0,2:T(8,128)S(1)} %copy-done, f32[32,1024]{1,0:T(8,128)S(1)} %add_divide_fusion), kind=kOutput, calls=%fused_computation.19 | convolution fusion | flops 2416115712 | bytes 5898240 | tf_op jit(solution)/shard_map/dot_general | solution.py:67
  156.8 0.9 convolution_bitcast_fusion
  157.7 2.9 %fusion.48 = (f32[6,32,1024]{2,1,0:T(8,128)S(1)}, f32[6,32,1024]{2,1,0:T(8,128)S(1)}) fusion(f32[6,32,1024]{2,1,0:T(8,128)S(1)} %fusion.20, f32[6]{0:T(128)S(1)} %compare_convert_fusion, f32[6,32,1024]{2,1,0:T(8,128)S(1)} %convolution_bitcast_fusion, f32[1024,1024,1]{1,0,2:T(8,128)S(1)} %copy-done), kind=kOutput, calls=%fused_computation.108 | convolution fusion | flops 2416312320 | bytes 7340056 | tf_op jit(solution)/shard_map/dot_general | solution.py:67
  160.6 0.8 reduce-precision_convert_fusion.1
  161.5 7.1 %fusion = f32[6,96,1024]{2,1,0:T(8,128)S(1)} fusion(s32[6,1024]{1,0:T(8,128)S(1)} %broadcast_subtract_fusion, s32[1024]{0:T(1024)S(1)} %get-tuple-element.30, s32[6,1024]{1,0:T(8,128)S(1)} %broadcast_subtract_fusion.1, s32[1024]{0:T(1024)S(1)} %get-tuple-element.31, bf16[6,32,1024]{2,1,0:T(8,128)(2,1)S(1)} %get-tuple-element.15, ...), kind=kOutput, calls=%fused_computation.4 | convolution fusion | flops 1230372864 | bytes 3596288 | tf_op jit(solution)/shard_map/pxc,pcy->pxy/dot_general | solution.py:56
  168.6 0.3 broadcast_select_fusion.1
  168.8 3.2 %collective-permute-start.2 = (f32[6,32,1024]{2,1,0:T(8,128)S(1)}, f32[6,32,1024]{2,1,0:T(8,128)S(1)}, u32[]{:S(2)}, u32[]{:S(2)}) collective-permute-start(f32[6,32,1024]{2,1,0:T(8,128)S(1)} %get-tuple-element.13), channel_id=1, source_target_pairs={{0,32},{32,64},{64,96},{96,128},{128,160},{160,192},{192,224},{224... | collective-permute-start | bytes 2359304 | tf_op jit(solution)/shard_map/ppermute | solution.py:14
  172.1 3.1 %collective-permute-start = (s32[6]{0:T(128)S(1)}, s32[6]{0:T(128)S(1)}, u32[]{:S(2)}, u32[]{:S(2)}) collective-permute-start(s32[6]{0:T(128)S(1)} %get-tuple-element.22), channel_id=1, source_target_pairs={{0,32},{32,64},{64,96},{96,128},{128,160},{160,192},{192,224},{224... | collective-permute-start | bytes 80 | tf_op jit(solution)/shard_map/ppermute | solution.py:14
  175.2 13.4 %collective-permute-done = s32[6]{0:T(128)S(1)} collective-permute-done((s32[6]{0:T(128)S(1)}, s32[6]{0:T(128)S(1)}, u32[]{:S(2)}, u32[]{:S(2)}) %collective-permute-start) | collective-permute-done | bytes 56 | tf_op jit(solution)/shard_map/ppermute | solution.py:14
  188.7 0.1 pad_add_fusion
  188.7 0.1 iota_compare_fusion.5
  188.8 0.0 collective-permute-done.2
  188.8 0.3 pad_maximum_fusion
  189.1 18.2 %select_reduce_fusion = f32[32,32,1024]{2,1,0:T(8,128)} fusion(f32[18,32,1024]{2,1,0:T(8,128)S(1)} %pad_maximum_fusion, pred[18,32]{1,0:T(8,128)(4,1)S(1)} %iota_compare_fusion.5), kind=kLoop, calls=%fused_computation.2 | loop fusion | flops 36700160 | bytes 6554176 | tf_op jit(solution)/shard_map/reduce_sum | solution.py:84
  207.3 57.0 %all_to_all.5 = f32[32,32,1024]{2,1,0:T(8,128)} all-to-all(f32[32,32,1024]{2,1,0:T(8,128)} %select_reduce_fusion), channel_id=1, replica_groups=mesh['grp'=16,'wrk'=32] {'wrk'}, dimensions={0} | all-to-all | bytes 8388608 | tf_op jit(solution)/shard_map/all_to_all | solution.py:129
  264.3 3.1 %reduce_sum.39 = f32[32,1024]{1,0:T(8,128)} reduce(f32[32,32,1024]{2,1,0:T(8,128)} %all_to_all.5, f32[]{:T(128)} %constant.85.clone.1), dimensions={0}, to_apply=%region_3.5 | reduce | flops 1015808 | bytes 4325380 | tf_op jit(solution)/shard_map/reduce_sum | solution.py:130
  (16 shorter events, 0.2 us)
Async XLA Ops:
  6.5 68.6 %all-gather.3.cloned.1.call-start = ((), (), s32[]{:S(2)}) async-start(), calls=%async_computation.1 | async-start | bytes 2162688 | tf_op jit(solution)/shard_map/all_gather | solution.py:92
  7.3 129.3 %all-gather.5.cloned.1.call-start = ((), (), s32[]{:S(2)}) async-start(), calls=%async_computation.2 | async-start | bytes 2162688 | tf_op jit(solution)/shard_map/all_gather | solution.py:93
  7.3 6.2 %collective-permute-start.1 = (bf16[1,32,1024]{2,1,0:T(8,128)(2,1)}, bf16[1,32,1024]{2,1,0:T(8,128)(2,1)S(1)}, u32[]{:S(2)}, u32[]{:S(2)}) collective-permute-start(bf16[1,32,1024]{2,1,0:T(8,128)(2,1)} %param.6), channel_id=1, source_target_pairs={{32,0},{64,32},{96,64},{128,96},{160,128},{192,160},{224,192},{256... | collective-permute-start | bytes 196616 | tf_op jit(solution)/shard_map/ppermute | solution.py:14
  13.5 0.6 copy-start.1
  22.2 15.0 %copy-start.3 = (s32[1,1,6,2]{2,3,1,0:T(2,128)S(1)}, s32[1,1,6,2]{2,3,1,0:T(2,128)}, u32[]{:S(2)}) copy-start(s32[1,1,6,2]{2,3,1,0:T(2,128)} %param.8) | copy-start | bytes 148
  22.2 15.1 %copy-start.2 = (s32[512,3]{0,1:T(4,128)S(1)}, s32[512,3]{0,1:T(4,128)}, u32[]{:S(2)}) copy-start(s32[512,3]{0,1:T(4,128)} %param.7) | copy-start | bytes 18436
  145.3 8.6 %copy-start = (f32[1024,1024,1]{1,0,2:T(8,128)S(1)}, f32[1024,1024,1]{1,0,2:T(8,128)}, u32[]{:S(2)}) copy-start(f32[1024,1024,1]{1,0,2:T(8,128)} %reshape.409) | copy-start | bytes 12582916
  168.8 20.0 %collective-permute-start.2 = (f32[6,32,1024]{2,1,0:T(8,128)S(1)}, f32[6,32,1024]{2,1,0:T(8,128)S(1)}, u32[]{:S(2)}, u32[]{:S(2)}) collective-permute-start(f32[6,32,1024]{2,1,0:T(8,128)S(1)} %get-tuple-element.13), channel_id=1, source_target_pairs={{0,32},{32,64},{64,96},{96,128},{128,160},{160,192},{192,224},{224... | collective-permute-start | bytes 2359304 | tf_op jit(solution)/shard_map/ppermute | solution.py:14
  172.1 16.6 %collective-permute-start = (s32[6]{0:T(128)S(1)}, s32[6]{0:T(128)S(1)}, u32[]{:S(2)}, u32[]{:S(2)}) collective-permute-start(s32[6]{0:T(128)S(1)} %get-tuple-element.22), channel_id=1, source_target_pairs={{0,32},{32,64},{64,96},{96,128},{128,160},{160,192},{192,224},{224... | collective-permute-start | bytes 80 | tf_op jit(solution)/shard_map/ppermute | solution.py:14
Sparse Core Ops, SparseCore 0:
  10.5 64.5 all-gather.2
  78.2 58.3 all-gather.4
where the time goes:
time: 275 us; the launch traced here: 274 us
  waiting for transfers between devices  114 us (41%)
  blocking collectives  57 us (21%)
  other arithmetic  30.8 us (11%)
  local copies, waits for them, and re-layouts  26.8 us (10%)
  matrix products  23.2 us (8%)
  between operations  14.3 us (5%)
  starting transfers between devices  7.69 us (3%)
    all_gather x1, waiting for transfers between devices, local(): lax.all_gather(passed_along(orbitals, 'grp', -1), 'wrk', axis=0, tiled=True)  58.3 us
    all_to_all x1, blocking collectives, local(): pieces = lax.all_to_all(combined, 'wrk', 0, 0, tiled=True)  57 us
    all_gather x1, waiting for transfers between devices, local(): own_set = lax.all_gather(orbitals, 'wrk', axis=0, tiled=True)  37.2 us
    reduce_sum x1, other arithmetic, rows_to_orbitals(): jnp.sum(jnp.where(chosen[:, :, None, None], fields[:, None, :, :], 0.0),...  18.2 us
    ppermute x3, waiting for transfers between devices, passed_along(): lax.ppermute(value, axis, [(source, source + steps) for source in range(i...  18.2 us
    mul x1, local copies, waits for them, and re-layouts, local(): sine_rows[:, None, :, None] * sine_rows[None, :, None, :]  13.7 us
    mul x1, other arithmetic, local(): sine_rows[:, None, :, None] * sine_rows[None, :, None, :]  8 us
    ppermute x3, starting transfers between devices, passed_along(): lax.ppermute(value, axis, [(source, source + steps) for source in range(i...  7.65 us
  transfers between devices with their start and end apart: 5, of which 4 were waited for; matrix products, arithmetic and copies ran while one was open for 10% of the time, Pallas kernels for 0%

commit v1 on v0

--- a/solution.py
+++ b/solution.py
@@ -6,6 +6,12 @@
 screen_shift = 0.05
 highest = lax.Precision.HIGHEST
 EXCHANGE = "all_to_all"
+
+
+def floor_remake(mine_x, axis_name):
+    return jnp.concatenate(
+        lax.all_to_all(jnp.stack([mine_x] * lax.axis_size(axis_name)), axis_name, 0, 0), axis=0
+    )
 
 
 def passed_along(value, axis, steps):
@@ -89,7 +95,7 @@
     workers = lax.axis_size("wrk")
     group_index = lax.axis_index("grp")
     grp_orbs = orb_dev * workers
-    own_set = lax.all_gather(orbitals, "wrk", axis=0, tiled=True)
+    own_set = floor_remake(orbitals, "wrk")
     upper_set = lax.all_gather(passed_along(orbitals, "grp", -1), "wrk", axis=0, tiled=True)
     group_set = jnp.concatenate([own_set, upper_set], axis=0)
     pair_list = pair_slots[0, 0]

time: 275 us -> 227 us (0.83)
  waiting for transfers between devices: 114 us -> 55.8 us
  starting transfers between devices: 7.69 us -> 18.3 us
  local copies, waits for them, and re-layouts: 26.8 us -> 22.8 us
  other arithmetic: 30.8 us -> 34.7 us
    all_gather x1 -> x0, waiting for transfers between devices: 37.2 us -> none  [local(): own_set = lax.all_gather(orbitals, 'wrk', axis=0, tiled=True)]
    all_gather x1, waiting for transfers between devices: 58.3 us -> 38.5 us  [local(): lax.all_gather(passed_along(orbitals, 'grp', -1), 'wrk', axis=0, tiled=True)]
    all_to_all x0 -> x1, starting transfers between devices: none -> 10.5 us  [floor_remake(): lax.all_to_all(jnp.stack([mine_x] * lax.axis_size(axis_name)), axis_name,...]
    ppermute x3, waiting for transfers between devices: 18.2 us -> 13.4 us  [passed_along(): lax.ppermute(value, axis, [(source, source + steps) for source in range(i...]
    concatenate x0 -> x1, other arithmetic: none -> 3.9 us  [local(): group_set = jnp.concatenate([own_set, upper_set], axis=0)]
    all_to_all x0 -> x1, waiting for transfers between devices: none -> 3.81 us  [floor_remake(): lax.all_to_all(jnp.stack([mine_x] * lax.axis_size(axis_name)), axis_name,...]
    unnamed x9 -> x8, local copies, waits for them, and re-layouts: 3.85 us -> 0.64 us
    concatenate x1 -> x0, local copies, waits for them, and re-layouts: 3.19 us -> none  [local(): group_set = jnp.concatenate([own_set, upper_set], axis=0)]
  transfers between devices with their start and end apart: 5 -> 5, of which waited for: 4 -> 3; matrix products, arithmetic and copies ran while one was open for 10% -> 11% of each run, Pallas kernels for 0% -> 0%
where the time goes in v1:
time: 227 us; the launch traced here: 226 us
  blocking collectives  57 us (25%)
  waiting for transfers between devices  55.8 us (25%)
  other arithmetic  34.7 us (15%)
  matrix products  23.1 us (10%)
  local copies, waits for them, and re-layouts  22.8 us (10%)
  starting transfers between devices  18.3 us (8%)
  between operations  14.3 us (6%)
    all_to_all x1, blocking collectives, local(): pieces = lax.all_to_all(combined, 'wrk', 0, 0, tiled=True)  57 us
    all_gather x1, waiting for transfers between devices, local(): lax.all_gather(passed_along(orbitals, 'grp', -1), 'wrk', axis=0, tiled=True)  38.5 us
    reduce_sum x1, other arithmetic, rows_to_orbitals(): jnp.sum(jnp.where(chosen[:, :, None, None], fields[:, None, :, :], 0.0),...  18.2 us
    mul x1, local copies, waits for them, and re-layouts, local(): sine_rows[:, None, :, None] * sine_rows[None, :, None, :]  13.7 us
    ppermute x3, waiting for transfers between devices, passed_along(): lax.ppermute(value, axis, [(source, source + steps) for source in range(i...  13.4 us
    all_to_all x1, starting transfers between devices, floor_remake(): lax.all_to_all(jnp.stack([mine_x] * lax.axis_size(axis_name)), axis_name,...  10.5 us
    mul x1, other arithmetic, local(): sine_rows[:, None, :, None] * sine_rows[None, :, None, :]  7.99 us
    ppermute x3, starting transfers between devices, passed_along(): lax.ppermute(value, axis, [(source, source + steps) for source in range(i...  7.78 us
  transfers between devices with their start and end apart: 5, of which 3 were waited for; matrix products, arithmetic and copies ran while one was open for 11% of the time, Pallas kernels for 0%

profile of v1, /device:TPU:1, one launch (start us, length us, event | category | flops | bytes accessed | tf_op | source)
XLA Modules:
  0.0 226.0 jit_solution(15299299111658692111)
XLA Ops:
  6.5 0.0 copy-start.3
  6.5 0.0 copy-start.2
  6.5 1.4 collective-permute-start.1
  8.0 2.4 %stack.2 = bf16[32,1,32,1024]{3,2,1,0:T(8,128)(2,1)} broadcast(bf16[32,1024]{1,0:T(8,128)(2,1)} %bitcast.40), dimensions={2,3} | broadcast | bytes 2162688 | tf_op jit(solution)/shard_map/stack | solution.py:13
  10.4 10.5 %all-to-all-start = ((bf16[32,1,32,1024]{3,2,1,0:T(8,128)(2,1)}), bf16[32,1,32,1024]{3,2,1,0:T(8,128)(2,1)S(1)}, u32[]{:S(2)}, u32[]{:S(2)}) async-start(bf16[32,1,32,1024]{3,2,1,0:T(8,128)(2,1)} %stack.2), calls=%async_computation | async-start | bytes 4194304 | tf_op jit(solution)/shard_map/all_to_all | solution.py:13
  20.9 0.0 all-gather.2.cloned.1.call-start
  21.0 0.0 copy-done.3
  21.0 0.0 collective-permute-done.1
  21.1 0.0 copy-start.1
  21.1 0.6 copy-done.1
  21.7 0.0 all-gather.2.cloned.1.call-update
  22.4 0.1 iota_compare_fusion.3
  22.5 0.0 copy-done.2
  22.5 0.2 select_reduce_fusion.1
  22.7 0.1 broadcast_add_fusion
  22.8 0.1 sine_multiply_fusion
  22.9 8.0 %broadcast_multiply_fusion = f32[32,32,32,32]{3,2,1,0:T(8,128)} fusion(f32[32,32]{1,0:T(8,128)S(1)} %sine_multiply_fusion), kind=kLoop, calls=%fused_computation.14 | loop fusion | flops 1048576 | bytes 4198400 | tf_op jit(solution)/shard_map/mul | solution.py:115
  30.9 13.7 %reshape.416 = f32[1024,1024,1]{1,0,2:T(8,128)} reshape(f32[32,32,32,32]{3,2,1,0:T(8,128)} %broadcast_multiply_fusion) | data formatting | bytes 8388608 | tf_op jit(solution)/shard_map/mul | solution.py:115
  44.6 0.2 add.123
  44.8 0.2 add.124
  45.0 0.1 add.125
  45.2 0.1 iota_subtract_fusion
  45.2 0.1 broadcast_subtract_fusion
  45.3 0.1 broadcast_subtract_fusion.1
  45.4 3.8 %all-to-all-done = bf16[32,1,32,1024]{3,2,1,0:T(8,128)(2,1)S(1)} async-done(((bf16[32,1,32,1024]{3,2,1,0:T(8,128)(2,1)}), bf16[32,1,32,1024]{3,2,1,0:T(8,128)(2,1)S(1)}, u32[]{:S(2)}, u32[]{:S(2)}) %all-to-all-start) | async-done | bytes 2097184 | tf_op jit(solution)/shard_map/all_to_all | solution.py:13
  49.2 38.5 %all-gather.2.cloned.1.call-done = bf16[32,32,1024]{2,1,0:T(8,128)(2,1)} async-done(((bf16[1,32,1024]{2,1,0:T(8,128)(2,1)}), bf16[32,32,1024]{2,1,0:T(8,128)(2,1)}) %all-gather.2.cloned.1.call-update) | async-done | bytes 2097168 | tf_op jit(solution)/shard_map/all_gather | solution.py:99
  87.7 3.9 %pad_maximum_fusion = bf16[64,32,1024]{2,1,0:T(8,128)(2,1)} fusion(bf16[32,32,1024]{2,1,0:T(8,128)(2,1)} %all-gather.2.cloned.1.call-done, bf16[32,32,1024]{2,1,0:T(8,128)(2,1)S(1)} %bitcast.39), kind=kLoop, calls=%fused_computation.15 | loop fusion | flops 2097152 | bytes 8388608 | tf_op jit(solution)/shard_map/concatenate | solution.py:100
  91.6 2.8 %gather_fusion.1 = bf16[6,32,1024]{2,1,0:T(8,128)(2,1)S(1)} fusion(bf16[64,32,1024]{2,1,0:T(8,128)(2,1)} %pad_maximum_fusion, s32[1024]{0:T(1024)S(1)} %pad_clamp_fusion), kind=kCustom, calls=%fused_computation.1.clone | custom fusion | bytes 786456 | tf_op jit(solution)/shard_map/jit(_take)/gather | solution.py:111
  94.4 2.8 %gather_fusion = bf16[6,32,1024]{2,1,0:T(8,128)(2,1)S(1)} fusion(bf16[64,32,1024]{2,1,0:T(8,128)(2,1)} %pad_maximum_fusion, s32[1024]{0:T(1024)S(1)} %pad_clamp_fusion.1), kind=kCustom, calls=%fused_computation.clone | custom fusion | bytes 786456 | tf_op jit(solution)/shard_map/jit(_take)/gather | solution.py:110
  97.2 0.0 copy-start
  97.2 7.0 %fusion.1 = f32[6,32,1024]{2,1,0:T(8,128)S(1)} fusion(s32[6,1024]{1,0:T(8,128)S(1)} %broadcast_subtract_fusion, s32[1024]{0:T(1024)S(1)} %get-tuple-element.30, s32[6,1024]{1,0:T(8,128)S(1)} %broadcast_subtract_fusion.1, s32[1024]{0:T(1024)S(1)} %get-tuple-element.31, bf16[6,32,1024]{2,1,0:T(8,128)(2,1)S(1)} %gather_fusion.1, ...), kind=kOutput, calls=%fused_computation.5 | convolution fusion | flops 421724160 | bytes 1236998 | tf_op jit(solution)/shard_map/pxc,pyc->pxy/dot_general | solution.py:51
  104.2 0.5 fusion.20
  104.7 1.0 convolution_bitcast_fusion.1
  105.7 0.0 copy-done
  105.7 2.9 %convolution_multiply_fusion.1 = f32[6,32,1024]{2,1,0:T(8,128)S(1)} fusion(f32[6,32,1024]{2,1,0:T(8,128)S(1)} %convolution_bitcast_fusion.1, f32[1024,1024,1]{1,0,2:T(8,128)S(1)} %copy-done, f32[32,1024]{1,0:T(8,128)S(1)} %add_divide_fusion), kind=kOutput, calls=%fused_computation.20 | convolution fusion | flops 2416115712 | bytes 5898240 | tf_op jit(solution)/shard_map/dot_general | solution.py:73
  108.6 0.9 convolution_bitcast_fusion
  109.6 2.9 %fusion.48 = (f32[6,32,1024]{2,1,0:T(8,128)S(1)}, f32[6,32,1024]{2,1,0:T(8,128)S(1)}) fusion(f32[6,32,1024]{2,1,0:T(8,128)S(1)} %fusion.20, f32[6]{0:T(128)S(1)} %compare_convert_fusion, f32[6,32,1024]{2,1,0:T(8,128)S(1)} %convolution_bitcast_fusion, f32[1024,1024,1]{1,0,2:T(8,128)S(1)} %copy-done), kind=kOutput, calls=%fused_computation.107 | convolution fusion | flops 2416312320 | bytes 7340056 | tf_op jit(solution)/shard_map/dot_general | solution.py:73
  112.5 0.8 reduce-precision_convert_fusion.1
  113.3 7.1 %fusion = f32[6,96,1024]{2,1,0:T(8,128)S(1)} fusion(s32[6,1024]{1,0:T(8,128)S(1)} %broadcast_subtract_fusion, s32[1024]{0:T(1024)S(1)} %get-tuple-element.30, s32[6,1024]{1,0:T(8,128)S(1)} %broadcast_subtract_fusion.1, s32[1024]{0:T(1024)S(1)} %get-tuple-element.31, bf16[6,32,1024]{2,1,0:T(8,128)(2,1)S(1)} %get-tuple-element.15, ...), kind=kOutput, calls=%fused_computation.4 | convolution fusion | flops 1230372864 | bytes 3596288 | tf_op jit(solution)/shard_map/pxc,pcy->pxy/dot_general | solution.py:62
  120.4 0.3 broadcast_select_fusion.1
  120.7 3.2 %collective-permute-start.2 = (f32[6,32,1024]{2,1,0:T(8,128)S(1)}, f32[6,32,1024]{2,1,0:T(8,128)S(1)}, u32[]{:S(2)}, u32[]{:S(2)}) collective-permute-start(f32[6,32,1024]{2,1,0:T(8,128)S(1)} %get-tuple-element.13), channel_id=1, source_target_pairs={{0,32},{32,64},{64,96},{96,128},{128,160},{160,192},{192,224},{224... | collective-permute-start | bytes 2359304 | tf_op jit(solution)/shard_map/ppermute | solution.py:20
  123.9 3.1 %collective-permute-start = (s32[6]{0:T(128)S(1)}, s32[6]{0:T(128)S(1)}, u32[]{:S(2)}, u32[]{:S(2)}) collective-permute-start(s32[6]{0:T(128)S(1)} %get-tuple-element.22), channel_id=1, source_target_pairs={{0,32},{32,64},{64,96},{96,128},{128,160},{160,192},{192,224},{224... | collective-permute-start | bytes 80 | tf_op jit(solution)/shard_map/ppermute | solution.py:20
  127.0 13.4 %collective-permute-done = s32[6]{0:T(128)S(1)} collective-permute-done((s32[6]{0:T(128)S(1)}, s32[6]{0:T(128)S(1)}, u32[]{:S(2)}, u32[]{:S(2)}) %collective-permute-start) | collective-permute-done | bytes 56 | tf_op jit(solution)/shard_map/ppermute | solution.py:20
  140.5 0.1 pad_add_fusion
  140.6 0.1 iota_compare_fusion.5
  140.6 0.0 collective-permute-done.2
  140.6 0.2 pad_maximum_fusion.1
  140.9 18.2 %select_reduce_fusion = f32[32,32,1024]{2,1,0:T(8,128)} fusion(f32[18,32,1024]{2,1,0:T(8,128)S(1)} %pad_maximum_fusion.1, pred[18,32]{1,0:T(8,128)(4,1)S(1)} %iota_compare_fusion.5), kind=kLoop, calls=%fused_computation.2 | loop fusion | flops 36700160 | bytes 6554176 | tf_op jit(solution)/shard_map/reduce_sum | solution.py:90
  159.1 57.0 %all_to_all.10 = f32[32,32,1024]{2,1,0:T(8,128)} all-to-all(f32[32,32,1024]{2,1,0:T(8,128)} %select_reduce_fusion), channel_id=1, replica_groups=mesh['grp'=16,'wrk'=32] {'wrk'}, dimensions={0} | all-to-all | bytes 8388608 | tf_op jit(solution)/shard_map/all_to_all | solution.py:135
  216.1 3.1 %reduce_sum.39 = f32[32,1024]{1,0:T(8,128)} reduce(f32[32,32,1024]{2,1,0:T(8,128)} %all_to_all.10, f32[]{:T(128)} %constant.85.clone.1), dimensions={0}, to_apply=%region_3.5 | reduce | flops 1015808 | bytes 4325380 | tf_op jit(solution)/shard_map/reduce_sum | solution.py:136
  (16 shorter events, 0.2 us)
Async XLA Ops:
  6.5 14.4 %copy-start.3 = (s32[1,1,6,2]{2,3,1,0:T(2,128)S(1)}, s32[1,1,6,2]{2,3,1,0:T(2,128)}, u32[]{:S(2)}) copy-start(s32[1,1,6,2]{2,3,1,0:T(2,128)} %param.8) | copy-start | bytes 148
  6.5 16.0 %copy-start.2 = (s32[512,3]{0,1:T(4,128)S(1)}, s32[512,3]{0,1:T(4,128)}, u32[]{:S(2)}) copy-start(s32[512,3]{0,1:T(4,128)} %param.7) | copy-start | bytes 18436
  6.5 14.5 %collective-permute-start.1 = (bf16[1,32,1024]{2,1,0:T(8,128)(2,1)}, bf16[1,32,1024]{2,1,0:T(8,128)(2,1)S(1)}, u32[]{:S(2)}, u32[]{:S(2)}) collective-permute-start(bf16[1,32,1024]{2,1,0:T(8,128)(2,1)} %param.6), channel_id=1, source_target_pairs={{32,0},{64,32},{96,64},{128,96},{160,128},{192,160},{224,192},{256... | collective-permute-start | bytes 196616 | tf_op jit(solution)/shard_map/ppermute | solution.py:20
  10.4 38.8 %all-to-all-start = ((bf16[32,1,32,1024]{3,2,1,0:T(8,128)(2,1)}), bf16[32,1,32,1024]{3,2,1,0:T(8,128)(2,1)S(1)}, u32[]{:S(2)}, u32[]{:S(2)}) async-start(bf16[32,1,32,1024]{3,2,1,0:T(8,128)(2,1)} %stack.2), calls=%async_computation | async-start | bytes 4194304 | tf_op jit(solution)/shard_map/all_to_all | solution.py:13
  20.9 66.8 %all-gather.2.cloned.1.call-start = ((), (), s32[]{:S(2)}) async-start(), calls=%async_computation.2 | async-start | bytes 2162688 | tf_op jit(solution)/shard_map/all_gather | solution.py:99
  21.1 0.6 copy-start.1
  97.2 8.5 %copy-start = (f32[1024,1024,1]{1,0,2:T(8,128)S(1)}, f32[1024,1024,1]{1,0,2:T(8,128)}, u32[]{:S(2)}) copy-start(f32[1024,1024,1]{1,0,2:T(8,128)} %reshape.416) | copy-start | bytes 12582916
  120.7 20.0 %collective-permute-start.2 = (f32[6,32,1024]{2,1,0:T(8,128)S(1)}, f32[6,32,1024]{2,1,0:T(8,128)S(1)}, u32[]{:S(2)}, u32[]{:S(2)}) collective-permute-start(f32[6,32,1024]{2,1,0:T(8,128)S(1)} %get-tuple-element.13), channel_id=1, source_target_pairs={{0,32},{32,64},{64,96},{96,128},{128,160},{160,192},{192,224},{224... | collective-permute-start | bytes 2359304 | tf_op jit(solution)/shard_map/ppermute | solution.py:20
  123.9 16.6 %collective-permute-start = (s32[6]{0:T(128)S(1)}, s32[6]{0:T(128)S(1)}, u32[]{:S(2)}, u32[]{:S(2)}) collective-permute-start(s32[6]{0:T(128)S(1)} %get-tuple-element.22), channel_id=1, source_target_pairs={{0,32},{32,64},{64,96},{96,128},{128,160},{160,192},{192,224},{224... | collective-permute-start | bytes 80 | tf_op jit(solution)/shard_map/ppermute | solution.py:20
Sparse Core Ops, SparseCore 0:
  24.9 62.8 all-gather.1
